TPU v7x, 256 devices: a whole 4x4x8 slice. The times are simulated.
256 devices in a mesh: blocks: 64 (over z, x, core), chan: 4 (over y).
Axes of the slice: x: 4, y: 4, z: 8, core: 2. Of those that a mesh axis runs over, the one named last changes fastest.
Arguments:
- fine_input: bfloat16 [1024, 64, 512], P('blocks', 'chan'), may hold values from -6 to 6
- block_counts: int32 [64], replicated, may hold values from 8 to 16, as said below
- fine_weight: bfloat16 [7, 64, 64], P(None, 'chan'), may hold values from -0.25 to 0.25
- fine_bias: float32 [64], P('chan'), may hold values from -3 to 3
- coarse_weight: bfloat16 [7, 64, 64], P(None, 'chan'), may hold values from -0.25 to 0.25
- coarse_bias: float32 [64], P('chan'), may hold values from -3 to 3
- coarse_cotangent: bfloat16 [128, 64, 512], P('blocks', 'chan'), may hold values from -48 to 48
Outputs:
- coarser_level_output: bfloat16 [128, 64, 512], P('blocks', 'chan')
- fine_grad: bfloat16 [1024, 64, 512], P('blocks', 'chan')
- fine_weight_grad: float32 [7, 64, 64], P(None, 'chan')
- fine_bias_grad: float32 [64], P('chan')
- coarse_weight_grad: float32 [7, 64, 64], P(None, 'chan')
- coarse_bias_grad: float32 [64], P('chan')
Inputs may be any that keep to these rules, and one draw needn't show every extreme that they name: `block_counts`: fine blocks held by each device of blocks; they sum to 768, and some device holds exactly 16.
All inputs are finite; a program needn't handle non-finite values.
Results may differ from a plain program's by a relative error of at most 0.017.
Values may be sent and summed in bfloat16 or wider, within the bound.
No kernel may reach another device: no remote copies, remote signals or barrier semaphores. Data moves between devices by JAX's collectives and lax.ppermute only.
A program may use at most 64 MiB of HBM per device.

v0:
```python
import jax
import jax.numpy as jnp
from jax import lax
from jax.sharding import PartitionSpec as P

EDGE = 8


TAP_PAIRS = (0, 2, 1, 4, 3, 6, 5)


def from_behind(block, axis, distance):
    devices = range(lax.axis_size(axis))
    route = [(i - distance, i) for i in devices if i - distance in devices]
    return lax.ppermute(block, axis, route)


def block_layers(block_cube):
    channels, edge_cells = (block_cube.shape[0], block_cube.shape[1])
    side_layers = [
        block_cube[:, :, :, 0],
        block_cube[:, :, :, -1],
        block_cube[:, :, 0, :],
        block_cube[:, :, -1, :],
        block_cube[:, 0],
        block_cube[:, -1],
    ]
    return jnp.stack(side_layers).reshape(6, channels, edge_cells * edge_cells)


def block_views(block_cube, halo_layers):
    channels, edge_cells = (block_cube.shape[0], block_cube.shape[1])
    sheets = halo_layers.reshape(6, channels, edge_cells, edge_cells)
    minus_x = jnp.concatenate([sheets[0][:, :, :, None], block_cube[:, :, :, :-1]], axis=3)
    plus_x = jnp.concatenate([block_cube[:, :, :, 1:], sheets[1][:, :, :, None]], axis=3)
    minus_y = jnp.concatenate([sheets[2][:, :, None, :], block_cube[:, :, :-1, :]], axis=2)
    plus_y = jnp.concatenate([block_cube[:, :, 1:, :], sheets[3][:, :, None, :]], axis=2)
    minus_z = jnp.concatenate([sheets[4][:, None], block_cube[:, :-1]], axis=1)
    plus_z = jnp.concatenate([block_cube[:, 1:], sheets[5][:, None]], axis=1)
    stacked = jnp.stack([block_cube, minus_x, plus_x, minus_y, plus_y, minus_z, plus_z])
    return stacked.reshape(7 * channels, edge_cells**3)


def slope_of(pre_values):
    sigmoid_values = jax.nn.sigmoid(pre_values)
    return sigmoid_values * (1.0 + pre_values * (1.0 - sigmoid_values))


def fine_halo(layer_table, block_ids, first_block, live_count, total_blocks):
    slot_count = layer_table.shape[0]
    plus_side = layer_table[:, 1::2]
    minus_side = layer_table[:, 0::2]
    tail_layers = lax.dynamic_slice_in_dim(plus_side, live_count - 4, 4, 0)
    from_lower = from_behind(tail_layers, "blocks", 1)
    from_upper = from_behind(minus_side[:4], "blocks", -1)
    table_minus = jnp.concatenate([from_lower, plus_side], axis=0)
    table_plus = jnp.concatenate([minus_side, from_upper], axis=0)
    strides = jnp.array([1, 2, 4], jnp.int32)
    lower_ids = block_ids[:, None] - strides[None, :]
    upper_octant_index = block_ids[:, None] + strides[None, :]
    end_block = first_block + live_count
    rows_minus = jnp.clip(lower_ids - first_block + 4, 0, slot_count + 3)
    rows_plus = jnp.clip(
        jnp.where(
            upper_octant_index < end_block,
            upper_octant_index - first_block,
            slot_count + upper_octant_index - end_block,
        ),
        0,
        slot_count + 3,
    )
    columns = jnp.arange(3, dtype=jnp.int32)[None, :]
    got_minus = table_minus[rows_minus, columns]
    got_plus = table_plus[rows_plus, columns]
    parity_x = block_ids % 2
    parity_y = block_ids // 2 % 2
    keep_minus = jnp.stack([parity_x == 1, parity_y == 1, block_ids >= 4], axis=1)
    keep_plus = jnp.stack([parity_x == 0, parity_y == 0, block_ids + 4 < total_blocks], axis=1)
    zero_value = jnp.zeros((), layer_table.dtype)
    got_minus = jnp.where(keep_minus[:, :, None, None], got_minus, zero_value)
    got_plus = jnp.where(keep_plus[:, :, None, None], got_plus, zero_value)
    merged = jnp.stack([got_minus, got_plus], axis=2)
    return merged.reshape(layer_table.shape)


def coarse_halo(layer_table, coarse_ids, coarse_first, coarse_count, coarse_total):
    slot_count = layer_table.shape[0]
    top_layers = layer_table[:, 5]
    bottom_layers = layer_table[:, 4]
    last_top = lax.dynamic_index_in_dim(top_layers, coarse_count - 1, 0, keepdims=False)
    from_lower = from_behind(last_top, "blocks", 1)
    from_upper = from_behind(bottom_layers[0], "blocks", -1)
    table_minus = jnp.concatenate([from_lower[None], top_layers], axis=0)
    table_plus = jnp.concatenate([bottom_layers, from_upper[None]], axis=0)
    rows_minus = jnp.clip(coarse_ids - coarse_first, 0, slot_count)
    rows_plus = jnp.clip(
        jnp.where(
            coarse_ids + 1 < coarse_first + coarse_count, coarse_ids + 1 - coarse_first, slot_count
        ),
        0,
        slot_count,
    )
    zero_value = jnp.zeros((), layer_table.dtype)
    below_layer = jnp.where((coarse_ids >= 1)[:, None, None], table_minus[rows_minus], zero_value)
    above_layer = jnp.where(
        (coarse_ids + 1 < coarse_total)[:, None, None], table_plus[rows_plus], zero_value
    )
    flat_zero = jnp.zeros_like(below_layer)
    return jnp.stack([flat_zero, flat_zero, flat_zero, flat_zero, below_layer, above_layer], axis=1)


def apply_blocks(matrix, block_cubes, halo_table):

    def one_block(operands):
        return jnp.dot(
            matrix, block_views(operands[0], operands[1]), preferred_element_type=jnp.float32
        )

    return lax.map(one_block, (block_cubes, halo_table))


def weight_block(operands):
    tap_views = block_views(operands[0], operands[1])
    return lax.dot_general(
        operands[2], tap_views, (((1,), (1,)), ((), ())), preferred_element_type=jnp.float32
    )


def restrict_blocks(hidden, half_edge):
    count, width = (hidden.shape[0], hidden.shape[1])
    shaped = hidden.reshape(count, width, half_edge, 2, half_edge, 2, half_edge, 2)
    return (
        (jnp.sum(shaped, axis=(3, 5, 7), dtype=jnp.float32) * 0.125)
        .astype(jnp.bfloat16)
        .reshape(count, width, half_edge**3)
    )


def local(
    fine_input, block_counts, fine_weight, fine_bias, coarse_weight, coarse_bias, coarse_cotangent
):
    slot_count, group_size, cell_count = fine_input.shape
    coarse_slots = coarse_cotangent.shape[0]
    channels = fine_weight.shape[2]
    half_edge = EDGE // 2
    octant_cells = half_edge**3
    pair_index = jnp.array(TAP_PAIRS, jnp.int32)
    device = lax.axis_index("blocks")
    starts = jnp.cumsum(block_counts) - block_counts
    first_block = starts[device]
    live_count = block_counts[device]
    end_block = first_block + live_count
    total_blocks = jnp.sum(block_counts)
    coarse_total = total_blocks // 8
    coarse_first = (first_block + 7) // 8
    coarse_count = (end_block + 7) // 8 - coarse_first
    block_ids = first_block + jnp.arange(slot_count, dtype=jnp.int32)
    coarse_ids = coarse_first + jnp.arange(coarse_slots, dtype=jnp.int32)
    live_mask = (jnp.arange(slot_count) < live_count)[:, None, None]
    coarse_live = (jnp.arange(coarse_slots) < coarse_count)[:, None, None]
    full_input = lax.all_gather(fine_input, "chan", axis=1, tiled=True)
    fine_cubes = full_input.reshape(slot_count, channels, EDGE, EDGE, EDGE)
    input_halos = fine_halo(
        jax.vmap(block_layers)(fine_cubes), block_ids, first_block, live_count, total_blocks
    )
    forward_fine = fine_weight.transpose(1, 0, 2).reshape(group_size, 7 * channels)
    pre_fine = apply_blocks(forward_fine, fine_cubes, input_halos) + fine_bias[None, :, None]
    octants = restrict_blocks(jax.nn.silu(pre_fine).astype(jnp.bfloat16), half_edge)
    upper_octants = from_behind(octants[:7], "blocks", -1)
    octant_table = jnp.concatenate([octants, upper_octants], axis=0)
    children = coarse_ids[:, None] * 8 + jnp.arange(8, dtype=jnp.int32)[None, :]
    child_rows = jnp.clip(
        jnp.where(children < end_block, children - first_block, slot_count + children - end_block),
        0,
        slot_count + 6,
    )
    gathered = octant_table[child_rows]
    coarse_local = (
        gathered.reshape(coarse_slots, 2, 2, 2, group_size, half_edge, half_edge, half_edge)
        .transpose(0, 4, 1, 5, 2, 6, 3, 7)
        .reshape(coarse_slots, group_size, cell_count)
    )
    coarse_local = jnp.where(coarse_live, coarse_local, jnp.zeros((), jnp.bfloat16))
    coarse_full = lax.all_gather(coarse_local, "chan", axis=1, tiled=True)
    coarse_cubes = coarse_full.reshape(coarse_slots, channels, EDGE, EDGE, EDGE)
    coarse_in_halos = coarse_halo(
        jax.vmap(block_layers)(coarse_cubes), coarse_ids, coarse_first, coarse_count, coarse_total
    )
    coarser_level_views = jax.vmap(block_views)(coarse_cubes, coarse_in_halos)
    forward_coarser_level = coarse_weight.transpose(1, 0, 2).reshape(group_size, 7 * channels)
    pre_coarse = (
        jnp.einsum(
            "ln,enp->elp",
            forward_coarser_level,
            coarser_level_views,
            preferred_element_type=jnp.float32,
        )
        + coarse_bias[None, :, None]
    )
    coarser_level_output = jnp.where(coarse_live, jax.nn.silu(pre_coarse), 0.0).astype(jnp.bfloat16)
    coarser_level_delta = jnp.where(
        coarse_live, coarse_cotangent.astype(jnp.float32) * slope_of(pre_coarse), 0.0
    ).astype(jnp.bfloat16)
    coarse_weight_grad = jnp.einsum(
        "zlc,znc->ln", coarser_level_delta, coarser_level_views, preferred_element_type=jnp.float32
    )
    coarse_weight_grad = coarse_weight_grad.reshape(group_size, 7, channels).transpose(1, 0, 2)
    coarse_bias_grad = jnp.sum(coarser_level_delta, axis=(0, 2), dtype=jnp.float32)
    coarse_weight_grad, coarse_bias_grad = lax.psum(
        (coarse_weight_grad, coarse_bias_grad), "blocks"
    )
    delta_cubes = coarser_level_delta.reshape(coarse_slots, group_size, EDGE, EDGE, EDGE)
    delta_halos = coarse_halo(
        jax.vmap(block_layers)(delta_cubes), coarse_ids, coarse_first, coarse_count, coarse_total
    )
    delta_window_views = jax.vmap(block_views)(delta_cubes, delta_halos)
    backward_coarser_level = (
        coarse_weight[pair_index].transpose(2, 0, 1).reshape(channels, 7 * group_size)
    )
    partial_sums = jnp.einsum(
        "ur,mre->mue",
        backward_coarser_level,
        delta_window_views,
        preferred_element_type=jnp.float32,
    )
    coarse_back = lax.psum_scatter(
        partial_sums.astype(jnp.bfloat16), "chan", scatter_dimension=1, tiled=True
    ).astype(jnp.float32)
    coarse_back = jnp.where(coarse_live, coarse_back, 0.0).astype(jnp.bfloat16)
    coarse_octants = (
        coarse_back.reshape(coarse_slots, group_size, 2, half_edge, 2, half_edge, 2, half_edge)
        .transpose(0, 2, 4, 6, 1, 3, 5, 7)
        .reshape(coarse_slots * 8, group_size, octant_cells)
    )
    last_octants = lax.dynamic_slice_in_dim(coarse_octants, (coarse_count - 1) * 8 + 1, 7, 0)
    lower_octants = from_behind(last_octants, "blocks", 1)
    back_table = jnp.concatenate([coarse_octants, lower_octants], axis=0)
    parents = block_ids // 8
    octant_ids = block_ids % 8
    back_rows = jnp.clip(
        jnp.where(
            parents >= coarse_first,
            (parents - coarse_first) * 8 + octant_ids,
            coarse_slots * 8 + octant_ids - 1,
        ),
        0,
        coarse_slots * 8 + 6,
    )
    picked_rows = back_table[back_rows]
    picked = picked_rows.reshape(slot_count, group_size, half_edge, 1, half_edge, 1, half_edge, 1)
    widened = jnp.broadcast_to(
        picked, (slot_count, group_size, half_edge, 2, half_edge, 2, half_edge, 2)
    ).reshape(slot_count, group_size, cell_count)
    fine_delta = jnp.where(
        live_mask, widened.astype(jnp.float32) * 0.125 * slope_of(pre_fine), 0.0
    ).astype(jnp.bfloat16)
    fine_weight_grad = jnp.sum(lax.map(weight_block, (fine_cubes, input_halos, fine_delta)), axis=0)
    fine_weight_grad = fine_weight_grad.reshape(group_size, 7, channels).transpose(1, 0, 2)
    fine_bias_grad = jnp.sum(fine_delta, axis=(0, 2), dtype=jnp.float32)
    fine_delta_cubes = fine_delta.reshape(slot_count, group_size, EDGE, EDGE, EDGE)
    fine_delta_halos = fine_halo(
        jax.vmap(block_layers)(fine_delta_cubes), block_ids, first_block, live_count, total_blocks
    )
    back_fine = fine_weight[pair_index].transpose(2, 0, 1).reshape(channels, 7 * group_size)
    fine_partial = apply_blocks(back_fine, fine_delta_cubes, fine_delta_halos)
    fine_back = lax.psum_scatter(
        fine_partial.astype(jnp.bfloat16), "chan", scatter_dimension=1, tiled=True
    ).astype(jnp.float32)
    fine_grad = jnp.where(live_mask, fine_back, 0.0).astype(jnp.bfloat16)
    fine_weight_grad, fine_bias_grad = lax.psum((fine_weight_grad, fine_bias_grad), "blocks")
    fine_norm = jnp.sqrt(total_blocks.astype(jnp.float32) * cell_count)
    coarse_norm = jnp.sqrt(coarse_total.astype(jnp.float32) * cell_count)
    return (
        coarser_level_output,
        fine_grad,
        fine_weight_grad / fine_norm,
        fine_bias_grad / fine_norm,
        coarse_weight_grad / coarse_norm,
        coarse_bias_grad / coarse_norm,
    )


def solution(mesh):
    placed = (
        P("blocks", "chan", None),
        P(),
        P(None, "chan", None),
        P("chan"),
        P(None, "chan", None),
        P("chan"),
        P("blocks", "chan", None),
    )
    return jax.shard_map(
        local,
        mesh=mesh,
        in_specs=placed,
        out_specs=(
            P("blocks", "chan", None),
            P("blocks", "chan", None),
            P(None, "chan", None),
            P("chan"),
            P(None, "chan", None),
            P("chan"),
        ),
        check_vma=False,
    )
```

profile of v0, /device:TPU:128, one launch (start us, length us, event | category | flops | bytes accessed | tf_op | source)
XLA Modules:
  0.0 713.2 jit_solution(11151267962573468808)
XLA Ops:
  7.2 1.8 copy.601
  26.2 12.4 %all-gather.2.cloned.1.call-done = bf16[16,64,512]{2,0,1:T(8,128)(2,1)} async-done(((bf16[16,16,512]{2,0,1:T(8,128)(2,1)}), bf16[16,64,512]{2,0,1:T(8,128)(2,1)}) %all-gather.2.cloned.1.call-update) | async-done | bytes 1048592 | tf_op jit(solution)/shard_map/all_gather | solution.py:161
  38.6 3.1 copy.602
  41.8 3.4 fusion.74
  49.8 1.9 collective-permute-start
  52.8 7.0 collective-permute-start.1
  66.7 65.5 %while.33 = (s32[]{:T(128)}, f32[16,16,512]{2,1,0:T(8,128)}, bf16[16,64,8,8,8]{1,4,3,2,0:T(8,128)(2,1)}, bf16[16,6,64,64]{2,3,1,0:T(8,128)(2,1)S(1)}, bf16[16,448]{1,0:T(8,128)(2,1)S(1)}) while((s32[]{:T(128)}, f32[16,16,512]{2,1,0:T(8,128)}, bf16[16,64,8,8,8]{1,4,3,2,0:T(8,128)(2,1)}, bf16[16,6,64,64]{2,3,1,0:T(8,128)(2,1)S(1)}, ...), condition=%wide.region_3.4_spmd.clone, body=%wide.region_2.3_spmd.sunk.clone | while | flops 8126471 | bytes 5126805 | solution.py:119
  133.8 3.7 copy.613
  137.5 2.8 reduce_sum.46
  140.5 7.1 collective-permute-start.2
  150.2 12.0 %all_gather.7 = bf16[2,64,512]{2,1,0:T(8,128)(2,1)S(1)} all-gather(bf16[2,16,512]{2,1,0:T(8,128)(2,1)S(1)} %broadcast_select_fusion.4), channel_id=1, replica_groups=mesh['blocks'=64,'chan'=4] {'chan'}, dimensions={1}, use_global_device_ids=true | all-gather | bytes 163840 | tf_op jit(solution)/shard_map/all_gather | solution.py:184
  163.0 4.1 collective-permute-start.4
  167.1 2.1 collective-permute-start.3
  170.3 5.2 collective-permute-done.3
  177.6 4.3 copy.630
  187.8 1.9 collective-permute-start.6
  190.4 2.5 collective-permute-start.5
  197.0 2.0 collective-permute-done.5
  203.6 4.3 copy.649
  210.9 20.1 %reduce-scatter.3.cloned.1.call-done = bf16[2,16,512]{2,1,0:T(8,128)(2,1)} async-done(((bf16[2,64,512]{2,1,0:T(8,128)(2,1)}), bf16[2,16,512]{2,1,0:T(8,128)(2,1)}) %reduce-scatter.3.cloned.1.call-update) | async-done | bytes 32784 | tf_op jit(solution)/shard_map/reduce_scatter | solution.py:226
  232.1 2.1 collective-permute-start.7
  237.8 3.7 collective-permute-done.7
  242.5 2.3 broadcast_in_dim.237
  244.9 2.8 copy.657
  248.7 1.7 copy.658
  250.4 3.4 fusion.73
  258.3 2.1 collective-permute-start.8
  261.4 7.0 collective-permute-start.9
  273.6 98.3 %while.34 = (s32[]{:T(128)}, bf16[16,64,512]{2,0,1:T(8,128)(2,1)S(1)}, bf16[16,16,8,8,8]{1,4,3,2,0:T(8,128)(2,1)}, bf16[16,6,16,64]{3,2,1,0:T(8,128)(2,1)}, bf16[64,112]{1,0:T(8,128)(2,1)S(1)}) while((s32[]{:T(128)}, bf16[16,64,512]{2,0,1:T(8,128)(2,1)S(1)}, bf16[16,16,8,8,8]{1,4,3,2,0:T(8,128)(2,1)}, ...), condition=%wide.region_7.8_spmd.clone, body=%wide.region_6.7_spmd.sunk.clone | while | flops 7536647 | bytes 3061913 | solution.py:119
  373.1 76.9 %while.35 = (s32[]{:T(128)}, f32[16,16,448]{2,1,0:T(8,128)}, bf16[16,16,512]{2,1,0:T(8,128)(2,1)S(1)}, bf16[16,64,8,8,8]{1,4,3,2,0:T(8,128)(2,1)}, bf16[16,6,64,64]{2,3,1,0:T(8,128)(2,1)}) while((s32[]{:T(128)}, f32[16,16,448]{2,1,0:T(8,128)}, bf16[16,16,512]{2,1,0:T(8,128)(2,1)S(1)}, bf16[16,64,8,8,8]{1,4,3,2,0:T(8,128)(2,1)}, ...), condition=%wide.region_10.11_spmd.clone, body=%wide.region_9.10_spmd.sunk.clone | while | flops 8126471 | bytes 5194901 | solution.py:257
  451.1 251.4 %all-reduce.8 = (f32[7,16,64]{2,0,1:T(8,128)S(1)}, f32[16]{0:T(128)S(1)}, f32[7,16,64]{2,1,0:T(8,128)S(1)}, f32[16]{0:T(128)S(1)}) all-reduce(f32[7,16,64]{2,0,1:T(8,128)S(1)} %bitcast.593, f32[16]{0:T(128)S(1)} %copy-done.20, f32[7,16,64]{2,1,0:T(8,128)S(1)} %convolution_bitcast_fusion.3, ...), channel_id=1, replica_groups=mesh['blocks'=64,'chan'=4] {'blocks'}, use_global_device_ids=true, to_apply=%region_12.13 | all-reduce | flops 14368 | bytes 114944 | tf_op jit(solution)/shard_map/psum | solution.py:270
  704.8 1.8 select_convert_fusion
  (1140 shorter events, 307.3 us)
Async XLA Ops:
  7.2 31.5 %all-gather.2.cloned.1.call-start = ((), (), s32[]{:S(2)}) async-start(), calls=%async_computation.2 | async-start | bytes 1310720 | tf_op jit(solution)/shard_map/all_gather | solution.py:161
  9.0 221.9 %reduce-scatter.3.cloned.1.call-start = ((), (), s32[]{:S(2)}) async-start(), calls=%async_computation.3 | async-start | bytes 163840 | tf_op jit(solution)/shard_map/reduce_scatter | solution.py:226
  25.5 144.1 %copy-start.13 = (s32[1024]{0:T(1024)}, s32[1024]{0:T(1024)S(1)}, u32[]{:S(2)}) copy-start(s32[1024]{0:T(1024)S(1)} %pad_clamp_fusion.2) | copy-start | bytes 12292
  25.5 150.0 %copy-start.12 = (s32[1024]{0:T(1024)}, s32[1024]{0:T(1024)S(1)}, u32[]{:S(2)}) copy-start(s32[1024]{0:T(1024)S(1)} %pad_clamp_fusion.3) | copy-start | bytes 12292
  49.8 10.4 %collective-permute-start = (bf16[4,3,64,64]{3,2,1,0:T(8,128)(2,1)S(1)}, bf16[4,3,64,64]{3,2,1,0:T(8,128)(2,1)}, u32[]{:S(2)}, u32[]{:S(2)}) collective-permute-start(bf16[4,3,64,64]{3,2,1,0:T(8,128)(2,1)S(1)} %constant_dynamic-slice_fusion.9), channel_id=1, source_target_pairs={{0,4},{4,8},{8,12},{12,16},{16,20},{20,24},{24,28},{28,32},{32,36}... | collective-permute-start | bytes 294920 | tf_op jit(solution)/shard_map/ppermute | solution.py:15
  51.7 118.5 %copy-start.15 = (pred[2]{0:T(512)(128)(4,1)}, pred[2]{0:T(512)(128)(4,1)S(1)}, u32[]{:S(2)}) copy-start(pred[2]{0:T(512)(128)(4,1)S(1)} %get-tuple-element.353) | copy-start | bytes 10
  51.7 124.3 %copy-start.14 = (pred[2]{0:T(512)(128)(4,1)}, pred[2]{0:T(512)(128)(4,1)S(1)}, u32[]{:S(2)}) copy-start(pred[2]{0:T(512)(128)(4,1)S(1)} %get-tuple-element.354) | copy-start | bytes 10
  52.8 10.4 %collective-permute-start.1 = (bf16[4,3,64,64]{3,2,1,0:T(8,128)(2,1)}, bf16[4,3,64,64]{3,2,1,0:T(8,128)(2,1)}, u32[]{:S(2)}, u32[]{:S(2)}) collective-permute-start(bf16[4,3,64,64]{3,2,1,0:T(8,128)(2,1)} %slice.398), channel_id=1, source_target_pairs={{4,0},{8,4},{12,8},{16,12},{20,16},{24,20},{28,24},{32,28},{36,32}... | collective-permute-start | bytes 294920 | tf_op jit(solution)/shard_map/ppermute | solution.py:15
  66.6 65.5 %copy-start.16 = (f32[16]{0:T(128)S(1)}, f32[16]{0:T(128)}, u32[]{:S(2)}) copy-start(f32[16]{0:T(128)} %param.19) | copy-start | bytes 196
  132.2 5.3 copy-start
  137.5 10.2 %copy-start.10 = (bf16[7,16,64]{2,1,0:T(8,128)(2,1)S(1)}, bf16[7,16,64]{2,1,0:T(8,128)(2,1)}, u32[]{:S(2)}) copy-start(bf16[7,16,64]{2,1,0:T(8,128)(2,1)} %param.20) | copy-start | bytes 43012
  140.5 8.7 %collective-permute-start.2 = (bf16[7,16,64]{2,1,0:T(8,128)(2,1)S(1)}, bf16[7,16,64]{2,1,0:T(8,128)(2,1)S(1)}, u32[]{:S(2)}, u32[]{:S(2)}) collective-permute-start(bf16[7,16,64]{2,1,0:T(8,128)(2,1)S(1)} %copy.615), channel_id=1, source_target_pairs={{4,0},{8,4},{12,8},{16,12},{20,16},{24,20},{28,24},{32,28},{36,32}... | collective-permute-start | bytes 43016 | tf_op jit(solution)/shard_map/ppermute | solution.py:15
  147.6 35.4 %copy-start.21 = (pred[2]{0:T(512)(128)(4,1)}, pred[2]{0:T(512)(128)(4,1)S(1)}, u32[]{:S(2)}) copy-start(pred[2]{0:T(512)(128)(4,1)S(1)} %iota_compare_fusion.1) | copy-start | bytes 10
  163.0 6.6 collective-permute-start.4
  167.1 8.4 %collective-permute-start.3 = (bf16[64,64]{0,1:T(8,128)(2,1)S(1)}, bf16[64,64]{0,1:T(8,128)(2,1)S(1)}, u32[]{:S(2)}, u32[]{:S(2)}) collective-permute-start(bf16[64,64]{0,1:T(8,128)(2,1)S(1)} %dynamic-slice_bitcast_fusion.15), channel_id=1, source_target_pairs={{0,4},{4,8},{8,12},{12,16},{16,20},{20,24},{24,28},{28,32},{32,36}... | collective-permute-start | bytes 24584 | tf_op jit(solution)/shard_map/ppermute | solution.py:15
  184.8 3.0 copy-start.8
  187.8 7.7 %collective-permute-start.6 = (bf16[16,64]{0,1:T(8,128)(2,1)S(1)}, bf16[16,64]{0,1:T(8,128)(2,1)S(1)}, u32[]{:S(2)}, u32[]{:S(2)}) collective-permute-start(bf16[16,64]{0,1:T(8,128)(2,1)S(1)} %slice_bitcast_fusion.18), channel_id=1, source_target_pairs={{4,0},{8,4},{12,8},{16,12},{20,16},{24,20},{28,24},{32,28},{36,32}... | collective-permute-start | bytes 6152 | tf_op jit(solution)/shard_map/ppermute | solution.py:15
  190.4 4.8 copy-start.7
  190.4 8.7 %collective-permute-start.5 = (bf16[16,64]{1,0:T(8,128)(2,1)}, bf16[16,64]{1,0:T(8,128)(2,1)}, u32[]{:S(2)}, u32[]{:S(2)}) collective-permute-start(bf16[16,64]{1,0:T(8,128)(2,1)} %bitcast.118), channel_id=1, source_target_pairs={{0,4},{4,8},{8,12},{12,16},{16,20},{20,24},{24,28},{28,32},{32,36}... | collective-permute-start | bytes 6152 | tf_op jit(solution)/shard_map/ppermute | solution.py:15
  192.9 9.3 %copy-start.6 = (bf16[2,16,7,8,8]{1,4,3,2,0:T(8,128)(2,1)S(1)}, bf16[2,16,7,8,8]{1,4,3,2,0:T(8,128)(2,1)}, u32[]{:S(2)}) copy-start(bf16[2,16,7,8,8]{1,4,3,2,0:T(8,128)(2,1)} %get-tuple-element.320) | copy-start | bytes 86020
  207.9 23.0 %copy-start.22 = (pred[2]{0:T(512)(128)(4,1)S(1)}, pred[2]{0:T(512)(128)(4,1)}, u32[]{:S(2)}) copy-start(pred[2]{0:T(512)(128)(4,1)} %copy-done.21) | copy-start | bytes 10
  208.0 27.6 %copy-start.11 = (bf16[7,16,64]{2,1,0:T(8,128)(2,1)S(1)}, bf16[7,16,64]{2,1,0:T(8,128)(2,1)}, u32[]{:S(2)}) copy-start(bf16[7,16,64]{2,1,0:T(8,128)(2,1)} %param.18) | copy-start | bytes 43012
  210.2 494.6 %reduce-scatter.5.cloned.1.call-start = ((), (), s32[]{:S(2)}) async-start(), calls=%async_computation.4 | async-start | bytes 1310720 | tf_op jit(solution)/shard_map/reduce_scatter | solution.py:266
  232.1 9.4 %collective-permute-start.7 = (bf16[7,16,64]{1,2,0:T(8,128)(2,1)S(1)}, bf16[7,16,64]{1,2,0:T(8,128)(2,1)S(1)}, u32[]{:S(2)}, u32[]{:S(2)}) collective-permute-start(bf16[7,16,64]{1,2,0:T(8,128)(2,1)S(1)} %constant_dynamic-slice_fusion.7), channel_id=1, source_target_pairs={{0,4},{4,8},{8,12},{12,16},{16,20},{20,24},{24,28},{28,32},{32,36}... | collective-permute-start | bytes 43016 | tf_op jit(solution)/shard_map/ppermute | solution.py:15
  234.9 12.8 %copy-start.18 = (pred[16]{0:T(512)(128)(4,1)}, pred[16]{0:T(512)(128)(4,1)S(1)}, u32[]{:S(2)}) copy-start(pred[16]{0:T(512)(128)(4,1)S(1)} %iota_compare_fusion) | copy-start | bytes 52
  244.9 2.9 copy-start.4
  244.9 2.9 copy-start.17
  258.3 10.5 %collective-permute-start.8 = (bf16[4,3,16,64]{2,3,1,0:T(8,128)(2,1)S(1)}, bf16[4,3,16,64]{2,3,1,0:T(8,128)(2,1)}, u32[]{:S(2)}, u32[]{:S(2)}) collective-permute-start(bf16[4,3,16,64]{2,3,1,0:T(8,128)(2,1)S(1)} %constant_dynamic-slice_fusion.6), channel_id=1, source_target_pairs={{0,4},{4,8},{8,12},{12,16},{16,20},{20,24},{24,28},{28,32},{32,36}... | collective-permute-start | bytes 73736 | tf_op jit(solution)/shard_map/ppermute | solution.py:15
  261.4 10.1 %collective-permute-start.9 = (bf16[4,3,16,64]{2,3,1,0:T(8,128)(2,1)S(1)}, bf16[4,3,16,64]{2,3,1,0:T(8,128)(2,1)S(1)}, u32[]{:S(2)}, u32[]{:S(2)}) collective-permute-start(bf16[4,3,16,64]{2,3,1,0:T(8,128)(2,1)S(1)} %slice.436), channel_id=1, source_target_pairs={{4,0},{8,4},{12,8},{16,12},{20,16},{24,20},{28,24},{32,28},{36,32}... | collective-permute-start | bytes 73736 | tf_op jit(solution)/shard_map/ppermute | solution.py:15
  373.0 78.0 %copy-start.20 = (f32[16]{0:T(128)S(1)}, f32[16]{0:T(128)}, u32[]{:S(2)}) copy-start(f32[16]{0:T(128)} %get-tuple-element.268) | copy-start | bytes 196
  373.0 78.0 %copy-start.23 = (f32[16]{0:T(128)S(1)}, f32[16]{0:T(128)}, u32[]{:S(2)}) copy-start(f32[16]{0:T(128)} %get-tuple-element.266) | copy-start | bytes 196
  373.0 331.8 %copy-start.19 = (pred[16]{0:T(512)(128)(4,1)S(1)}, pred[16]{0:T(512)(128)(4,1)}, u32[]{:S(2)}) copy-start(pred[16]{0:T(512)(128)(4,1)} %copy-done.18) | copy-start | bytes 52
  (7 other events, 10.4 us)
Sparse Core Ops, SparseCore 0:
  10.4 28.2 all-gather.1
  210.3 20.5 reduce-scatter.2
  373.1 26.3 reduce-scatter.4
where the time goes:
time: 717 us; the launch traced here: 713 us
  blocking collectives  263 us (37%)
  local copies, waits for them, and re-layouts  261 us (36%)
  waiting for transfers between devices  46.4 us (6%)
  other arithmetic  46.4 us (6%)
  starting transfers between devices  37.9 us (5%)
  matrix products  32.3 us (5%)
  between operations  21.6 us (3%)
    psum x1, blocking collectives, local(): lax.psum((fine_weight_grad, fine_bias_grad), 'blocks')  251 us
    another operation x48, local copies, waits for them, and re-layouts, block_views(): jnp.stack([block_cube, minus_x, plus_x, minus_y, plus_y, minus_z, plus_z])  52.6 us
    squeeze x48, local copies, waits for them, and re-layouts, apply_blocks(): return lax.map(one_block, (block_cubes, halo_table))  45.5 us
    ppermute x10, starting transfers between devices, from_behind(): return lax.ppermute(block, axis, route)  37.8 us
    reshape x50, local copies, waits for them, and re-layouts, block_views(): return stacked.reshape(7 * channels, edge_cells ** 3)  28.9 us
    dynamic_update_slice x32, local copies, waits for them, and re-layouts, apply_blocks(): return lax.map(one_block, (block_cubes, halo_table))  20.9 us
    reduce_scatter x1, waiting for transfers between devices, local(): lax.psum_scatter(partial_sums.astype(jnp.bfloat16), 'chan', scatter_dimen...  20.1 us
    while x240, other arithmetic  17.3 us
  transfers between devices with their start and end apart: 13, of which 10 were waited for; matrix products, arithmetic and copies ran while one was open for 15% of the time, Pallas kernels for 0%

commit v1 on v0

--- a/solution.py
+++ b/solution.py
@@ -134,6 +134,22 @@
         .astype(jnp.bfloat16)
         .reshape(count, width, half_edge**3)
     )
+
+
+def sum_over_blocks(parts):
+    chan_index = lax.axis_index("chan")
+    chan_count = lax.axis_size("chan")
+    flat = jnp.concatenate([part.reshape(-1) for part in parts])
+    slots = jnp.zeros((chan_count, flat.shape[0]), flat.dtype)
+    slots = lax.dynamic_update_index_in_dim(slots, flat, chan_index, 0)
+    summed = lax.psum(slots, ("blocks", "chan"))
+    mine = lax.dynamic_index_in_dim(summed, chan_index, 0, keepdims=False)
+    pieces = []
+    offset = 0
+    for part in parts:
+        pieces.append(mine[offset : offset + part.size].reshape(part.shape))
+        offset += part.size
+    return tuple(pieces)
 
 
 def local(
@@ -164,7 +180,11 @@
         jax.vmap(block_layers)(fine_cubes), block_ids, first_block, live_count, total_blocks
     )
     forward_fine = fine_weight.transpose(1, 0, 2).reshape(group_size, 7 * channels)
-    pre_fine = apply_blocks(forward_fine, fine_cubes, input_halos) + fine_bias[None, :, None]
+    fine_views = jax.vmap(block_views)(fine_cubes, input_halos)
+    pre_fine = (
+        jnp.einsum("ln,bnp->blp", forward_fine, fine_views, preferred_element_type=jnp.float32)
+        + fine_bias[None, :, None]
+    )
     octants = restrict_blocks(jax.nn.silu(pre_fine).astype(jnp.bfloat16), half_edge)
     upper_octants = from_behind(octants[:7], "blocks", -1)
     octant_table = jnp.concatenate([octants, upper_octants], axis=0)
@@ -206,9 +226,6 @@
     )
     coarse_weight_grad = coarse_weight_grad.reshape(group_size, 7, channels).transpose(1, 0, 2)
     coarse_bias_grad = jnp.sum(coarser_level_delta, axis=(0, 2), dtype=jnp.float32)
-    coarse_weight_grad, coarse_bias_grad = lax.psum(
-        (coarse_weight_grad, coarse_bias_grad), "blocks"
-    )
     delta_cubes = coarser_level_delta.reshape(coarse_slots, group_size, EDGE, EDGE, EDGE)
     delta_halos = coarse_halo(
         jax.vmap(block_layers)(delta_cubes), coarse_ids, coarse_first, coarse_count, coarse_total
@@ -254,7 +271,9 @@
     fine_delta = jnp.where(
         live_mask, widened.astype(jnp.float32) * 0.125 * slope_of(pre_fine), 0.0
     ).astype(jnp.bfloat16)
-    fine_weight_grad = jnp.sum(lax.map(weight_block, (fine_cubes, input_halos, fine_delta)), axis=0)
+    fine_weight_grad = jnp.einsum(
+        "blp,bnp->ln", fine_delta, fine_views, preferred_element_type=jnp.float32
+    )
     fine_weight_grad = fine_weight_grad.reshape(group_size, 7, channels).transpose(1, 0, 2)
     fine_bias_grad = jnp.sum(fine_delta, axis=(0, 2), dtype=jnp.float32)
     fine_delta_cubes = fine_delta.reshape(slot_count, group_size, EDGE, EDGE, EDGE)
@@ -262,12 +281,17 @@
         jax.vmap(block_layers)(fine_delta_cubes), block_ids, first_block, live_count, total_blocks
     )
     back_fine = fine_weight[pair_index].transpose(2, 0, 1).reshape(channels, 7 * group_size)
-    fine_partial = apply_blocks(back_fine, fine_delta_cubes, fine_delta_halos)
+    fine_delta_views = jax.vmap(block_views)(fine_delta_cubes, fine_delta_halos)
+    fine_partial = jnp.einsum(
+        "ur,bre->bue", back_fine, fine_delta_views, preferred_element_type=jnp.float32
+    )
     fine_back = lax.psum_scatter(
         fine_partial.astype(jnp.bfloat16), "chan", scatter_dimension=1, tiled=True
     ).astype(jnp.float32)
     fine_grad = jnp.where(live_mask, fine_back, 0.0).astype(jnp.bfloat16)
-    fine_weight_grad, fine_bias_grad = lax.psum((fine_weight_grad, fine_bias_grad), "blocks")
+    fine_weight_grad, fine_bias_grad, coarse_weight_grad, coarse_bias_grad = sum_over_blocks(
+        (fine_weight_grad, fine_bias_grad, coarse_weight_grad, coarse_bias_grad)
+    )
     fine_norm = jnp.sqrt(total_blocks.astype(jnp.float32) * cell_count)
     coarse_norm = jnp.sqrt(coarse_total.astype(jnp.float32) * cell_count)
     return (

time: 717 us -> 580 us (0.81)
  blocking collectives: 263 us -> 12 us
  waiting for transfers between devices: 46.4 us -> 216 us
  local copies, waits for them, and re-layouts: 261 us -> 217 us
  matrix products: 32.3 us -> 19.2 us
    psum x1 -> x0, blocking collectives: 251 us -> none  [local(): lax.psum((fine_weight_grad, fine_bias_grad), 'blocks')]
    psum x0 -> x1, waiting for transfers between devices: none -> 161 us  [sum_over_blocks(): summed = lax.psum(slots, ('blocks', 'chan'))]
    transpose x2 -> x4, local copies, waits for them, and re-layouts: 8.6 us -> 75.6 us  [block_views(): return stacked.reshape(7 * channels, edge_cells ** 3)]
    another operation x49 -> x3, local copies, waits for them, and re-layouts: 53.3 us -> 3.19 us  [the longest x2 2.44 us: block_views(): sheets = halo_layers.reshape(6, channels, edge_cells, edge_cells)]
    squeeze x48 -> x0, local copies, waits for them, and re-layouts: 45.5 us -> none  [apply_blocks(): return lax.map(one_block, (block_cubes, halo_table))]
    reduce_scatter x1, waiting for transfers between devices: 0.01 us -> 25.1 us  [local(): lax.psum_scatter(fine_partial.astype(jnp.bfloat16), 'chan', scatter_dimen...]
    unnamed x2 -> x13, other arithmetic: 1.09 us -> 23.8 us
    dynamic_update_slice x32 -> x1, local copies, waits for them, and re-layouts: 20.9 us -> 1.23 us  [sum_over_blocks(): slots = lax.dynamic_update_index_in_dim(slots, flat, chan_index, 0)]
  transfers between devices with their start and end apart: 13 -> 14, of which waited for: 10 -> 8; matrix products, arithmetic and copies ran while one was open for 15% -> 21% of each run, Pallas kernels for 0% -> 0%
where the time goes in v1:
time: 580 us; the launch traced here: 571 us
  local copies, waits for them, and re-layouts  217 us (37%)
  waiting for transfers between devices  216 us (37%)
  other arithmetic  48.9 us (8%)
  starting transfers between devices  35.7 us (6%)
  between operations  21.9 us (4%)
  matrix products  19.2 us (3%)
  blocking collectives  12 us (2%)
    psum x1, waiting for transfers between devices, sum_over_blocks(): summed = lax.psum(slots, ('blocks', 'chan'))  161 us
    transpose x4, local copies, waits for them, and re-layouts, block_views(): return stacked.reshape(7 * channels, edge_cells ** 3)  75.6 us
    reshape x4, local copies, waits for them, and re-layouts, block_views(): return stacked.reshape(7 * channels, edge_cells ** 3)  41.7 us
    ppermute x10, starting transfers between devices, from_behind(): return lax.ppermute(block, axis, route)  35.5 us
    reduce_scatter x1, waiting for transfers between devices, local(): lax.psum_scatter(fine_partial.astype(jnp.bfloat16), 'chan', scatter_dimen...  25.1 us
    unnamed x13, other arithmetic  23.8 us
    dot_general x1, local copies, waits for them, and re-layouts, local(): jnp.einsum('blp,bnp->ln', fine_delta, fine_views, preferred_element_type=...  14.8 us
    ppermute x10, waiting for transfers between devices, from_behind(): return lax.ppermute(block, axis, route)  13.7 us
  transfers between devices with their start and end apart: 14, of which 8 were waited for; matrix products, arithmetic and copies ran while one was open for 21% of the time, Pallas kernels for 0%

profile of v1, /device:TPU:128, one launch (start us, length us, event | category | flops | bytes accessed | tf_op | source)
XLA Modules:
  0.0 570.5 jit_solution(10096941222904606873)
XLA Ops:
  26.3 12.3 %all-gather.2.cloned.1.call-done = bf16[16,64,512]{2,0,1:T(8,128)(2,1)} async-done(((bf16[16,16,512]{2,0,1:T(8,128)(2,1)}), bf16[16,64,512]{2,0,1:T(8,128)(2,1)}) %all-gather.2.cloned.1.call-update) | async-done | bytes 1048592 | tf_op jit(solution)/shard_map/all_gather | solution.py:177
  42.1 2.9 fusion.73
  45.0 2.9 fusion.72
  47.9 3.0 fusion.71
  53.5 7.0 %collective-permute-start.1 = (bf16[4,3,64,64]{2,3,1,0:T(8,128)(2,1)S(1)}, bf16[4,3,64,64]{2,3,1,0:T(8,128)(2,1)S(1)}, u32[]{:S(2)}, u32[]{:S(2)}) collective-permute-start(bf16[4,3,64,64]{2,3,1,0:T(8,128)(2,1)S(1)} %slice.370), channel_id=1, source_target_pairs={{4,0},{8,4},{12,8},{16,12},{20,16},{24,20},{28,24},{32,28},{36,32}... | collective-permute-start | bytes 294920 | tf_op jit(solution)/shard_map/ppermute | solution.py:15
  76.7 2.7 fusion.3
  87.3 33.5 %copy.344 = bf16[16,7,64,8,8,8]{2,1,5,4,3,0:T(8,128)(2,1)} copy(bf16[16,7,64,8,8,8]{2,5,4,3,0,1:T(8,128)(2,1)} %bitcast.418) | data formatting | bytes 14680064 | tf_op jit(solution)/shard_map/vmap()/transpose | solution.py:41
  120.8 22.2 %reshape.836 = bf16[16,448,512]{1,2,0:T(8,128)(2,1)} reshape(bf16[16,7,64,8,8,8]{2,1,5,4,3,0:T(8,128)(2,1)} %copy.344) | data formatting | bytes 14680064 | tf_op jit(solution)/shard_map/vmap()/reshape | solution.py:41
  143.1 6.5 %fusion.21 = (f32[16,16,512]{2,1,0:T(8,128)S(1)}, f32[16,16,512]{2,1,0:T(8,128)}) fusion(f32[16]{0:T(128)S(1)} %copy-done.27, bf16[16,448,512]{1,2,0:T(8,128)(2,1)} %reshape.836, bf16[16,448,1]{1,0,2:T(8,128)(2,1)S(1)} %reshape.951), kind=kOutput, calls=%fused_computation.62 | convolution fusion | flops 118358016 | bytes 8403008 | tf_op jit(solution)/shard_map/ln,bnp->blp/dot_general | solution.py:185
  149.6 3.7 copy.347
  153.3 2.8 reduce_sum.37
  156.3 5.2 collective-permute-start.2
  164.1 12.0 %all_gather.7 = bf16[2,64,512]{2,1,0:T(8,128)(2,1)S(1)} all-gather(bf16[2,16,512]{2,1,0:T(8,128)(2,1)S(1)} %broadcast_select_fusion.4), channel_id=1, replica_groups=mesh['blocks'=64,'chan'=4] {'chan'}, dimensions={1}, use_global_device_ids=true | all-gather | bytes 163840 | tf_op jit(solution)/shard_map/all_gather | solution.py:204
  176.8 4.1 collective-permute-start.4
  184.0 5.3 collective-permute-done.3
  191.4 4.3 copy.364
  218.0 4.3 copy.383
  227.0 14.8 %copy.416 = bf16[448,16,512]{2,1,0:T(8,128)(2,1)} copy(bf16[448,16,512]{0,2,1:T(8,128)(2,1)} %bitcast.416) | data formatting | bytes 14680064 | tf_op jit(solution)/shard_map/blp,bnp->ln/dot_general | solution.py:274
  242.3 3.8 reduce-scatter.3.cloned.1.call-done
  249.9 6.8 %collective-permute-done.7 = bf16[7,16,64]{1,2,0:T(8,128)(2,1)S(1)} collective-permute-done((bf16[7,16,64]{1,2,0:T(8,128)(2,1)S(1)}, bf16[7,16,64]{1,2,0:T(8,128)(2,1)S(1)}, u32[]{:S(2)}, u32[]{:S(2)}) %collective-permute-start.7) | collective-permute-done | bytes 14368 | tf_op jit(solution)/shard_map/ppermute | solution.py:15
  260.1 2.8 copy.391
  265.7 2.9 fusion.69
  268.6 2.9 fusion.68
  271.5 3.0 fusion.67
  274.5 7.7 %fusion.18 = f32[7,16,64]{2,1,0:T(8,128)S(1)} fusion(bf16[7,64,16,512]{3,2,1,0:T(8,128)(2,1)S(1)} %bitcast.441, bf16[16,16,512]{2,1,0:T(8,128)(2,1)S(1)} %get-tuple-element.11), kind=kOutput, calls=%fused_computation.49 | convolution fusion | flops 117440512 | bytes 7630848 | tf_op jit(solution)/shard_map/blp,bnp->ln/dot_general | solution.py:274
  288.1 7.0 %collective-permute-start.9 = (bf16[4,3,16,64]{2,3,1,0:T(8,128)(2,1)S(1)}, bf16[4,3,16,64]{2,3,1,0:T(8,128)(2,1)S(1)}, u32[]{:S(2)}, u32[]{:S(2)}) collective-permute-start(bf16[4,3,16,64]{2,3,1,0:T(8,128)(2,1)S(1)} %slice.420), channel_id=1, source_target_pairs={{4,0},{8,4},{12,8},{16,12},{20,16},{24,20},{28,24},{32,28},{36,32}... | collective-permute-start | bytes 73736 | tf_op jit(solution)/shard_map/ppermute | solution.py:15
  305.4 2.7 fusion.8
  308.1 2.7 fusion.9
  318.6 33.5 %copy.413 = bf16[16,7,16,8,8,8]{2,1,5,4,3,0:T(8,128)(2,1)} copy(bf16[16,7,16,8,8,8]{2,5,4,3,0,1:T(8,128)(2,1)} %bitcast.417) | data formatting | bytes 3670016 | tf_op jit(solution)/shard_map/vmap()/transpose | solution.py:41
  352.2 17.2 %reshape.852 = bf16[16,112,512]{1,2,0:T(8,128)(2,1)S(1)} reshape(bf16[16,7,16,8,8,8]{2,1,5,4,3,0:T(8,128)(2,1)} %copy.413) | data formatting | bytes 3670016 | tf_op jit(solution)/shard_map/vmap()/reshape | solution.py:41
  372.0 160.8 %all-reduce.10.cloned.1.call-done = f32[4,14368]{1,0:T(4,128)} async-done(((f32[4,14368]{1,0:T(4,128)}), f32[4,14368]{1,0:T(4,128)}) %all-reduce.10.cloned.1.call-update) | async-done | bytes 229904 | tf_op jit(solution)/shard_map/psum | solution.py:145
  536.6 25.1 %reduce-scatter.5.cloned.1.call-done = bf16[16,16,512]{2,1,0:T(8,128)(2,1)} async-done(((bf16[16,64,512]{2,1,0:T(8,128)(2,1)}), bf16[16,16,512]{2,1,0:T(8,128)(2,1)}) %reduce-scatter.5.cloned.1.call-update) | async-done | bytes 262160 | tf_op jit(solution)/shard_map/reduce_scatter | solution.py:288
  (300 shorter events, 120.1 us)
Async XLA Ops:
  7.2 31.4 %all-gather.2.cloned.1.call-start = ((), (), s32[]{:S(2)}) async-start(), calls=%async_computation.2 | async-start | bytes 1310720 | tf_op jit(solution)/shard_map/all_gather | solution.py:177
  9.0 237.1 %reduce-scatter.3.cloned.1.call-start = ((), (), s32[]{:S(2)}) async-start(), calls=%async_computation.3 | async-start | bytes 163840 | tf_op jit(solution)/shard_map/reduce_scatter | solution.py:243
  25.6 158.3 %copy-start.26 = (pred[2]{0:T(512)(128)(4,1)}, pred[2]{0:T(512)(128)(4,1)S(1)}, u32[]{:S(2)}) copy-start(pred[2]{0:T(512)(128)(4,1)S(1)} %get-tuple-element.81) | copy-start | bytes 10
  25.6 164.3 %copy-start.25 = (pred[2]{0:T(512)(128)(4,1)}, pred[2]{0:T(512)(128)(4,1)S(1)}, u32[]{:S(2)}) copy-start(pred[2]{0:T(512)(128)(4,1)S(1)} %get-tuple-element.82) | copy-start | bytes 10
  25.6 157.7 %copy-start.24 = (s32[1024]{0:T(1024)}, s32[1024]{0:T(1024)S(1)}, u32[]{:S(2)}) copy-start(s32[1024]{0:T(1024)S(1)} %pad_clamp_fusion.2) | copy-start | bytes 12292
  25.6 163.7 %copy-start.23 = (s32[1024]{0:T(1024)}, s32[1024]{0:T(1024)S(1)}, u32[]{:S(2)}) copy-start(s32[1024]{0:T(1024)S(1)} %pad_clamp_fusion.3) | copy-start | bytes 12292
  51.6 10.5 %collective-permute-start = (bf16[4,3,64,64]{2,3,1,0:T(8,128)(2,1)S(1)}, bf16[4,3,64,64]{2,3,1,0:T(8,128)(2,1)S(1)}, u32[]{:S(2)}, u32[]{:S(2)}) collective-permute-start(bf16[4,3,64,64]{2,3,1,0:T(8,128)(2,1)S(1)} %constant_dynamic-slice_fusion.3), channel_id=1, source_target_pairs={{0,4},{4,8},{8,12},{12,16},{16,20},{20,24},{24,28},{28,32},{32,36}... | collective-permute-start | bytes 294920 | tf_op jit(solution)/shard_map/ppermute | solution.py:15
  53.5 12.1 %collective-permute-start.1 = (bf16[4,3,64,64]{2,3,1,0:T(8,128)(2,1)S(1)}, bf16[4,3,64,64]{2,3,1,0:T(8,128)(2,1)S(1)}, u32[]{:S(2)}, u32[]{:S(2)}) collective-permute-start(bf16[4,3,64,64]{2,3,1,0:T(8,128)(2,1)S(1)} %slice.370), channel_id=1, source_target_pairs={{4,0},{8,4},{12,8},{16,12},{20,16},{24,20},{28,24},{32,28},{36,32}... | collective-permute-start | bytes 294920 | tf_op jit(solution)/shard_map/ppermute | solution.py:15
  76.7 2.7 copy-start.11
  120.8 22.2 %copy-start.27 = (f32[16]{0:T(128)S(1)}, f32[16]{0:T(128)}, u32[]{:S(2)}) copy-start(f32[16]{0:T(128)} %param.13) | copy-start | bytes 196
  153.3 8.2 %copy-start.21 = (bf16[7,16,64]{2,1,0:T(8,128)(2,1)S(1)}, bf16[7,16,64]{2,1,0:T(8,128)(2,1)}, u32[]{:S(2)}) copy-start(bf16[7,16,64]{2,1,0:T(8,128)(2,1)} %param.14) | copy-start | bytes 43012
  156.3 6.7 %collective-permute-start.2 = (bf16[7,16,64]{2,1,0:T(8,128)(2,1)S(1)}, bf16[7,16,64]{2,1,0:T(8,128)(2,1)S(1)}, u32[]{:S(2)}, u32[]{:S(2)}) collective-permute-start(bf16[7,16,64]{2,1,0:T(8,128)(2,1)S(1)} %copy.349), channel_id=1, source_target_pairs={{4,0},{8,4},{12,8},{16,12},{20,16},{24,20},{28,24},{32,28},{36,32}... | collective-permute-start | bytes 43016 | tf_op jit(solution)/shard_map/ppermute | solution.py:15
  161.5 35.3 %copy-start.28 = (pred[2]{0:T(512)(128)(4,1)}, pred[2]{0:T(512)(128)(4,1)S(1)}, u32[]{:S(2)}) copy-start(pred[2]{0:T(512)(128)(4,1)S(1)} %iota_compare_fusion.1) | copy-start | bytes 10
  176.8 6.5 %collective-permute-start.4 = (bf16[64,64]{0,1:T(8,128)(2,1)S(1)}, bf16[64,64]{0,1:T(8,128)(2,1)S(1)}, u32[]{:S(2)}, u32[]{:S(2)}) collective-permute-start(bf16[64,64]{0,1:T(8,128)(2,1)S(1)} %slice_bitcast_fusion.31), channel_id=1, source_target_pairs={{4,0},{8,4},{12,8},{16,12},{20,16},{24,20},{28,24},{32,28},{36,32}... | collective-permute-start | bytes 24584 | tf_op jit(solution)/shard_map/ppermute | solution.py:15
  180.9 8.4 %collective-permute-start.3 = (bf16[64,64]{0,1:T(8,128)(2,1)S(1)}, bf16[64,64]{0,1:T(8,128)(2,1)S(1)}, u32[]{:S(2)}, u32[]{:S(2)}) collective-permute-start(bf16[64,64]{0,1:T(8,128)(2,1)S(1)} %dynamic-slice_bitcast_fusion), channel_id=1, source_target_pairs={{0,4},{4,8},{8,12},{12,16},{16,20},{20,24},{24,28},{28,32},{32,36}... | collective-permute-start | bytes 24584 | tf_op jit(solution)/shard_map/ppermute | solution.py:15
  202.1 7.9 %collective-permute-start.6 = (bf16[16,64]{0,1:T(8,128)(2,1)}, bf16[16,64]{0,1:T(8,128)(2,1)}, u32[]{:S(2)}, u32[]{:S(2)}) collective-permute-start(bf16[16,64]{0,1:T(8,128)(2,1)} %slice_bitcast_fusion.30), channel_id=1, source_target_pairs={{4,0},{8,4},{12,8},{16,12},{20,16},{24,20},{28,24},{32,28},{36,32}... | collective-permute-start | bytes 6152 | tf_op jit(solution)/shard_map/ppermute | solution.py:15
  204.7 5.0 copy-start.19
  204.7 8.7 %collective-permute-start.5 = (bf16[16,64]{1,0:T(8,128)(2,1)}, bf16[16,64]{1,0:T(8,128)(2,1)}, u32[]{:S(2)}, u32[]{:S(2)}) collective-permute-start(bf16[16,64]{1,0:T(8,128)(2,1)} %bitcast.86), channel_id=1, source_target_pairs={{0,4},{4,8},{8,12},{12,16},{16,20},{20,24},{24,28},{28,32},{32,36}... | collective-permute-start | bytes 6152 | tf_op jit(solution)/shard_map/ppermute | solution.py:15
  207.4 9.2 %copy-start.18 = (bf16[2,16,7,8,8]{1,4,3,2,0:T(8,128)(2,1)S(1)}, bf16[2,16,7,8,8]{1,4,3,2,0:T(8,128)(2,1)}, u32[]{:S(2)}) copy-start(bf16[2,16,7,8,8]{1,4,3,2,0:T(8,128)(2,1)} %get-tuple-element.44) | copy-start | bytes 86020
  222.3 2.9 copy-start.22
  224.5 308.3 %all-reduce.10.cloned.1.call-start = ((), (), s32[]{:S(2)}) async-start(), calls=%async_computation.5 | async-start | bytes 462848 | tf_op jit(solution)/shard_map/psum | solution.py:145
  227.0 19.1 %copy-start.29 = (pred[2]{0:T(512)(128)(4,1)S(1)}, pred[2]{0:T(512)(128)(4,1)}, u32[]{:S(2)}) copy-start(pred[2]{0:T(512)(128)(4,1)} %copy-done.28) | copy-start | bytes 10
  247.3 9.4 %collective-permute-start.7 = (bf16[7,16,64]{1,2,0:T(8,128)(2,1)S(1)}, bf16[7,16,64]{1,2,0:T(8,128)(2,1)S(1)}, u32[]{:S(2)}, u32[]{:S(2)}) collective-permute-start(bf16[7,16,64]{1,2,0:T(8,128)(2,1)S(1)} %constant_dynamic-slice_fusion.1), channel_id=1, source_target_pairs={{0,4},{4,8},{8,12},{12,16},{16,20},{20,24},{24,28},{28,32},{32,36}... | collective-permute-start | bytes 43016 | tf_op jit(solution)/shard_map/ppermute | solution.py:15
  260.1 2.9 copy-start.14
  265.7 8.9 %slice-start = ((s8[7340032]{0:T(1024)(128)(4,1)}), s8[4194304]{0:T(1024)(128)(4,1)S(1)}, s32[]{:S(2)}) async-start(s8[7340032]{0:T(1024)(128)(4,1)} %bitcast.439), calls=%async_computation.6 | async-start | bytes 8388608
  268.6 5.9 %slice-start.1 = ((s8[7340032]{0:T(1024)(128)(4,1)}), s8[3145728]{0:T(1024)(128)(4,1)S(1)}, s32[]{:S(2)}) async-start(s8[7340032]{0:T(1024)(128)(4,1)} %bitcast.439), calls=%async_computation.7 | async-start | bytes 6291456
  274.5 7.8 %copy-start.30 = (f32[16]{0:T(128)S(1)}, f32[16]{0:T(128)}, u32[]{:S(2)}) copy-start(f32[16]{0:T(128)} %get-tuple-element.8) | copy-start | bytes 196
  284.5 277.3 %reduce-scatter.5.cloned.1.call-start = ((), (), s32[]{:S(2)}) async-start(), calls=%async_computation.4 | async-start | bytes 1310720 | tf_op jit(solution)/shard_map/reduce_scatter | solution.py:288
  286.1 12.3 %collective-permute-start.8 = (bf16[4,3,16,64]{2,3,1,0:T(8,128)(2,1)S(1)}, bf16[4,3,16,64]{2,3,1,0:T(8,128)(2,1)}, u32[]{:S(2)}, u32[]{:S(2)}) collective-permute-start(bf16[4,3,16,64]{2,3,1,0:T(8,128)(2,1)S(1)} %constant_dynamic-slice_fusion), channel_id=1, source_target_pairs={{0,4},{4,8},{8,12},{12,16},{16,20},{20,24},{24,28},{28,32},{32,36}... | collective-permute-start | bytes 73736 | tf_op jit(solution)/shard_map/ppermute | solution.py:15
  288.1 12.5 %collective-permute-start.9 = (bf16[4,3,16,64]{2,3,1,0:T(8,128)(2,1)S(1)}, bf16[4,3,16,64]{2,3,1,0:T(8,128)(2,1)S(1)}, u32[]{:S(2)}, u32[]{:S(2)}) collective-permute-start(bf16[4,3,16,64]{2,3,1,0:T(8,128)(2,1)S(1)} %slice.420), channel_id=1, source_target_pairs={{4,0},{8,4},{12,8},{16,12},{20,16},{24,20},{28,24},{32,28},{36,32}... | collective-permute-start | bytes 73736 | tf_op jit(solution)/shard_map/ppermute | solution.py:15
  308.1 2.7 copy-start.7
  352.1 17.2 %copy-start.20 = (bf16[7,16,64]{2,1,0:T(8,128)(2,1)S(1)}, bf16[7,16,64]{2,1,0:T(8,128)(2,1)}, u32[]{:S(2)}) copy-start(bf16[7,16,64]{2,1,0:T(8,128)(2,1)} %gather_fusion.11) | copy-start | bytes 43012
  (17 other events, 29.0 us)
Sparse Core Ops, SparseCore 0:
  10.4 28.2 all-gather.1
  224.6 21.4 reduce-scatter.2
  284.6 248.0 all-reduce.9
  535.2 26.5 reduce-scatter.4
